TPU v7x, 256 devices: a whole 4x4x8 slice. The times are simulated.
256 devices in a mesh: dp: 32 (over x, y, core), mp: 8 (over z).
Axes of the slice: x: 4, y: 4, z: 8, core: 2. Of those that a mesh axis runs over, the one named last changes fastest.
Arguments:
- hidden: bfloat16 [512, 1024], P('dp'), may hold values from -6 to 6
- attn_gain: float32 [1024], replicated, may hold values from 0.25 to 1.75
- w_qkv: bfloat16 [1024, 3, 1024], P(None, None, 'mp'), may hold values from -2 to 2
- w_out: bfloat16 [1024, 1024], P('mp'), may hold values from -0.1875 to 0.1875
- mlp_gain: float32 [1024], replicated, may hold values from 0.25 to 1.75
- w_gate_up: bfloat16 [1024, 2, 4096], P(None, None, 'mp'), may hold values from -0.1875 to 0.1875
- w_down: bfloat16 [4096, 1024], P('mp'), may hold values from -0.09375 to 0.09375
- kv_cache: bfloat16 [2, 4096, 128, 1024], P(None, 'dp', None, 'mp'), may hold values from -9 to 9
- lengths: int32 [512], replicated, may hold values from 1 to 16384, as said below
- page_request: int32 [4096], P('dp'), may hold values from -1 to 511, as said below
- page_index: int32 [4096], P('dp'), may hold values from 0 to 127, as said below
Outputs:
- appended: bfloat16 [2, 512, 1024], P(None, 'dp', 'mp')
- hidden_out: bfloat16 [512, 1024], P('dp')
Inputs may be any that keep to these rules, and one draw needn't show every extreme that they name: `lengths`: 4 requests hold exactly 16384 tokens, the others fewer than 512. `page_request`: each request owns exactly ceil(lengths / 128) pool pages, which may lie on any data devices; -1 marks an empty page. `page_index`: the pages of a request carry the places 0 to ceil(lengths / 128) - 1, each once; empty pages carry 0.
All inputs are finite; a program needn't handle non-finite values.
Results may differ from a plain program's by a relative error of at most 0.0085.
Values may be sent and summed in bfloat16 or wider, within the bound.
No kernel may reach another device: no remote copies, remote signals or barrier semaphores. Data moves between devices by JAX's collectives and lax.ppermute only.
A program may use at most 128 MiB of HBM per device.

v0:
```python
import jax
import jax.numpy as jnp
from jax import lax
from jax.sharding import PartitionSpec as P

HEAD_DIM = 64
EPSILON = 1e-05
NEGATIVE = -1e30


def rms_norm(values, gain):
    widened = values.astype(jnp.float32)
    mean_square = jnp.mean(widened * widened, axis=-1, keepdims=True)
    return (widened * lax.rsqrt(mean_square + EPSILON) * gain).astype(jnp.bfloat16)


def body(
    hidden,
    attn_gain,
    w_qkv,
    w_out,
    mlp_gain,
    w_gate_up,
    w_down,
    kv_cache,
    lengths,
    page_request,
    page_index,
):
    local_rows = hidden.shape[0]
    head_cols = w_qkv.shape[2]
    local_heads = head_cols // HEAD_DIM
    pool_pages = kv_cache.shape[1]
    page_len = kv_cache.shape[2]
    data_devices = lax.axis_size("dp")
    requests = local_rows * data_devices
    score_scale = HEAD_DIM ** (-0.5)
    normed = rms_norm(hidden, attn_gain)
    projected = jnp.dot(
        normed, w_qkv.reshape(w_qkv.shape[0], 3 * head_cols), preferred_element_type=jnp.float32
    )
    projected = lax.optimization_barrier(projected.astype(jnp.bfloat16)).reshape(
        local_rows, 3, head_cols
    )
    appended = jnp.stack([projected[:, 1], projected[:, 2]])
    every_query = lax.all_gather(projected[:, 0], "dp", axis=0, tiled=True)
    own_queries = projected[:, 0].reshape(local_rows, local_heads, HEAD_DIM).astype(jnp.float32)
    own_keys = projected[:, 1].reshape(local_rows, local_heads, HEAD_DIM).astype(jnp.float32)
    own_values = projected[:, 2].reshape(local_rows, local_heads, HEAD_DIM).astype(jnp.float32)
    self_scores = jnp.sum(own_queries * own_keys, axis=-1) * score_scale
    home_row = lax.axis_index("dp") * local_rows
    request_ids = jnp.arange(requests, dtype=jnp.int32)
    offsets = jnp.arange(page_len, dtype=jnp.int32)
    owners = page_request
    clamped = jnp.maximum(owners, 0)
    chosen_queries = every_query[clamped].reshape(pool_pages, local_heads, HEAD_DIM)
    key_rows = kv_cache[0].reshape(pool_pages, page_len, local_heads, HEAD_DIM)
    value_rows = kv_cache[1].reshape(pool_pages, page_len, local_heads, HEAD_DIM)
    scores = (
        jnp.einsum("phd,pthd->pht", chosen_queries, key_rows, preferred_element_type=jnp.float32)
        * score_scale
    )
    position = page_index[:, None] * page_len + offsets[None, :]
    usable = (owners[:, None] >= 0) & (position < lengths[clamped][:, None])
    page_max = jnp.max(jnp.where(usable[:, None, :], scores, NEGATIVE), axis=2)
    raw = jnp.where(usable[:, None, :], jnp.exp(scores - page_max[:, :, None]), 0.0)
    page_total = jnp.sum(raw, axis=2)
    page_sum = jnp.einsum(
        "pht,pthd->phd", raw.astype(jnp.bfloat16), value_rows, preferred_element_type=jnp.float32
    )
    member = owners[:, None] == request_ids[None, :]
    seg_max = jnp.max(jnp.where(member[:, :, None], page_max[:, None, :], NEGATIVE), axis=0)
    self_full = lax.dynamic_update_slice(
        jnp.full((requests, local_heads), NEGATIVE, jnp.float32), self_scores, (home_row, 0)
    )
    local_max = jnp.maximum(seg_max, self_full)
    factors = jnp.where(owners[:, None] >= 0, jnp.exp(page_max - local_max[clamped]), 0.0)
    payload = jnp.concatenate(
        [(page_sum * factors[:, :, None]).reshape(pool_pages, head_cols), page_total * factors],
        axis=1,
    )
    onehot = member.astype(jnp.float32)
    local_sums = jnp.einsum("pr,pc->rc", onehot, payload, precision=lax.Precision.HIGHEST)
    home_max = lax.dynamic_slice_in_dim(local_max, home_row, local_rows, 0)
    self_weight = jnp.exp(self_scores - home_max)
    self_payload = jnp.concatenate(
        [(self_weight[:, :, None] * own_values).reshape(local_rows, head_cols), self_weight], axis=1
    )
    local_sums = local_sums + lax.dynamic_update_slice(
        jnp.zeros_like(local_sums), self_payload, (home_row, 0)
    )
    global_max = lax.pmax(local_max, "dp")
    shrink = jnp.exp(local_max - global_max)
    shrink_cols = jnp.concatenate([jnp.repeat(shrink, HEAD_DIM, axis=1), shrink], axis=1)
    mine = lax.psum_scatter(local_sums * shrink_cols, "dp", scatter_dimension=0, tiled=True)
    own_weighted = mine[:, :head_cols].reshape(local_rows, local_heads, HEAD_DIM)
    own_totals = mine[:, head_cols:]
    context = (
        (own_weighted / own_totals[:, :, None]).reshape(local_rows, head_cols).astype(jnp.bfloat16)
    )
    attended = lax.psum(jnp.dot(context, w_out, preferred_element_type=jnp.float32), "mp")
    residual = lax.optimization_barrier(
        (hidden.astype(jnp.float32) + attended).astype(jnp.bfloat16)
    )
    normed_mlp = rms_norm(residual, mlp_gain)
    hidden_cols = w_gate_up.shape[2]
    gate_up = jnp.dot(
        normed_mlp,
        w_gate_up.reshape(w_gate_up.shape[0], 2 * hidden_cols),
        preferred_element_type=jnp.float32,
    ).reshape(local_rows, 2, hidden_cols)
    activated = (jax.nn.silu(gate_up[:, 0]) * gate_up[:, 1]).astype(jnp.bfloat16)
    lowered = lax.psum(jnp.dot(activated, w_down, preferred_element_type=jnp.float32), "mp")
    hidden_out = (residual.astype(jnp.float32) + lowered).astype(jnp.bfloat16)
    return (appended, hidden_out)


def solution(mesh):
    return jax.shard_map(
        body,
        mesh=mesh,
        in_specs=(
            P("dp", None),
            P(),
            P(None, None, "mp"),
            P("mp", None),
            P(),
            P(None, None, "mp"),
            P("mp", None),
            P(None, "dp", None, "mp"),
            P(),
            P("dp"),
            P("dp"),
        ),
        out_specs=(P(None, "dp", "mp"), P("dp", None)),
        check_vma=False,
    )
```

profile of v0, /device:TPU:2, one launch (start us, length us, event | category | flops | bytes accessed | tf_op | source)
XLA Modules:
  0.0 378.3 jit_solution(6640743451332159533)
XLA Ops:
  7.2 0.7 broadcast_maximum_fusion
  8.6 0.8 iota_compare_fusion
  9.4 1.4 copy.92
  10.8 0.9 fusion.9
  11.7 1.1 convolution_convert_fusion
  12.9 24.7 %all-gather = bf16[512,1,128]{2,0,1:T(8,128)(2,1)S(1)} all-gather(bf16[16,1,128]{2,0,1:T(8,128)(2,1)S(1)} %copy.95), channel_id=2, replica_groups=mesh['dp'=32,'mp'=8] {'dp'}, dimensions={0}, use_global_device_ids=true | all-gather | bytes 135168 | tf_op jit(solution)/shard_map/all_gather | solution.py:46
  38.6 6.0 %fusion.35 = (bf16[1,128,128,128]{3,2,1,0:T(8,128)(2,1)}, bf16[1,128,128,128]{3,2,1,0:T(8,128)(2,1)}) fusion(bf16[2,128,128,128]{3,2,1,0:T(8,128)(2,1)} %param.18), kind=kLoop, calls=%fused_computation.69 | loop fusion | bytes 16777216 | tf_op jit(solution)/shard_map/slice | solution.py:58
  44.6 6.4 %copy.111 = bf16[1,128,128,128]{2,3,1,0:T(8,128)(2,1)} copy(bf16[1,128,128,128]{3,2,1,0:T(8,128)(2,1)} %get-tuple-element.9) | data formatting | bytes 8388608
  51.0 1.3 gather_fusion
  52.3 3.4 fusion.37
  56.9 55.7 %pmax.7 = f32[512,2]{0,1:T(2,128)S(1)} all-reduce(f32[512,2]{0,1:T(2,128)S(1)} %max.9), channel_id=1, replica_groups=mesh['dp'=32,'mp'=8] {'dp'}, use_global_device_ids=true, to_apply=%region_5.6 | all-reduce | flops 1024 | bytes 8192 | tf_op jit(solution)/shard_map/pmax | solution.py:92
  113.3 6.4 %copy.112 = bf16[1,128,128,128]{2,3,1,0:T(8,128)(2,1)} copy(bf16[1,128,128,128]{3,2,1,0:T(8,128)(2,1)} %get-tuple-element.8) | data formatting | bytes 8388608
  119.7 4.6 %fusion = f32[128,2,1,64]{3,2,1,0:T(1,128)S(1)} fusion(bf16[128,128,2,64]{1,3,2,0:T(8,128)(2,1)} %bitcast.70, bf16[128,2,128,1]{2,0,1,3:T(8,128)(2,1)S(1)} %get-tuple-element.10), kind=kOutput, calls=%fused_computation.8 | convolution fusion | flops 4194304 | bytes 4325376 | tf_op jit(solution)/shard_map/pht,pthd->phd/dot_general | solution.py:68
  125.8 0.8 maximum_multiply_fusion
  126.5 1.9 copy.107
  128.6 92.6 %reduce-scatter.4.cloned.1.call-done = f32[16,130]{1,0:T(8,128)} async-done(((f32[512,130]{1,0:T(8,128)}), f32[16,130]{1,0:T(8,128)}) %reduce-scatter.4.cloned.1.call-update) | async-done | bytes 8336
  222.8 1.8 fusion.38
  224.7 1.9 copy.116
  226.6 2.9 copy.102
  229.5 67.3 %all-reduce.3.cloned.1.call-done = f32[16,1024]{1,0:T(8,128)} async-done(((f32[16,1024]{1,0:T(8,128)}), f32[16,1024]{1,0:T(8,128)}) %all-reduce.3.cloned.1.call-update) | async-done | bytes 65552 | tf_op jit(solution)/shard_map/psum | solution.py:101
  296.8 0.8 fusion.12
  298.4 0.9 fusion.29
  299.9 70.4 %all-reduce.5.cloned.1.call-done = f32[16,1024]{1,0:T(8,128)} async-done(((f32[16,1024]{1,0:T(8,128)}), f32[16,1024]{1,0:T(8,128)}) %all-reduce.5.cloned.1.call-update) | async-done | bytes 65552 | tf_op jit(solution)/shard_map/psum | solution.py:113
  370.3 1.5 fusion.16
  (66 shorter events, 8.2 us)
Async XLA Ops:
  7.2 291.2 %copy-start = (bf16[512,1024]{1,0:T(8,128)(2,1)S(1)}, bf16[512,1024]{1,0:T(8,128)(2,1)}, u32[]{:S(2)}) copy-start(bf16[512,1024]{1,0:T(8,128)(2,1)} %param.17) | copy-start | bytes 3145732
  7.2 214.0 %reduce-scatter.4.cloned.1.call-start = ((), (), s32[]{:S(2)}) async-start(), calls=%async_computation.3 | async-start | bytes 540672
  44.6 6.4 %copy-start.1 = (s32[512]{0:T(512)S(1)}, s32[512]{0:T(512)}, u32[]{:S(2)}) copy-start(s32[512]{0:T(512)} %param.19) | copy-start | bytes 6148
  44.6 7.7 %copy-start.6 = (s32[128]{0:T(128)S(1)}, s32[128]{0:T(128)}, u32[]{:S(2)}) copy-start(s32[128]{0:T(128)} %param.21) | copy-start | bytes 1540
  119.7 4.9 %copy-start.5 = (s32[128]{0:T(128)S(1)}, s32[128]{0:T(128)}, u32[]{:S(2)}) copy-start(s32[128]{0:T(128)} %param.20) | copy-start | bytes 1540
  119.7 104.9 %copy-start.2 = (bf16[1024,2,512]{2,1,0:T(2,128)(2,1)S(1)}, bf16[1024,2,512]{2,1,0:T(2,128)(2,1)}, u32[]{:S(2)}) copy-start(bf16[1024,2,512]{2,1,0:T(2,128)(2,1)} %param.16) | copy-start | bytes 6291460
  128.5 168.3 %all-reduce.3.cloned.1.call-start = ((), (), s32[]{:S(2)}) async-start(), calls=%async_computation.1 | async-start | bytes 131072 | tf_op jit(solution)/shard_map/psum | solution.py:101
  224.6 145.8 %all-reduce.5.cloned.1.call-start = ((), (), s32[]{:S(2)}) async-start(), calls=%async_computation.2 | async-start | bytes 131072 | tf_op jit(solution)/shard_map/psum | solution.py:113
  224.6 72.1 %copy-start.3 = (bf16[16,1024]{1,0:T(8,128)(2,1)S(1)}, bf16[16,1024]{1,0:T(8,128)(2,1)}, u32[]{:S(2)}) copy-start(bf16[16,1024]{1,0:T(8,128)(2,1)} %param.11) | copy-start | bytes 98308
  224.6 73.1 %copy-start.4 = (f32[1024]{0:T(1024)S(1)}, f32[1024]{0:T(1024)}, u32[]{:S(2)}) copy-start(f32[1024]{0:T(1024)} %param.15) | copy-start | bytes 12292
Sparse Core Ops, SparseCore 0:
  128.6 92.5 reduce-scatter.3
  224.7 72.0 all-reduce.2
  299.4 70.8 all-reduce.4
where the time goes:
time: 379 us; the launch traced here: 378 us
  waiting for transfers between devices  230 us (61%)
  blocking collectives  80.4 us (21%)
  local copies, waits for them, and re-layouts  32.9 us (9%)
  between operations  14 us (4%)
  matrix products  12.7 us (3%)
  other arithmetic  7.77 us (2%)
    unnamed x4, waiting for transfers between devices  92.7 us
    psum x1, waiting for transfers between devices, body(): lax.psum(jnp.dot(activated, w_down, preferred_element_type=jnp.float32),...  70.4 us
    psum x1, waiting for transfers between devices, body(): lax.psum(jnp.dot(context, w_out, preferred_element_type=jnp.float32), 'mp')  67.3 us
    pmax x1, blocking collectives, body(): global_max = lax.pmax(local_max, 'dp')  55.7 us
    all_gather x1, blocking collectives, body(): every_query = lax.all_gather(projected[:, 0], 'dp', axis=0, tiled=True)  24.7 us
    unnamed x22, local copies, waits for them, and re-layouts  18.4 us
  transfers between devices with their start and end apart: 3, of which 3 were waited for; matrix products, arithmetic and copies ran while one was open for 1% of the time, Pallas kernels for 0%

commit v1 on v0

--- a/solution.py
+++ b/solution.py
@@ -43,7 +43,9 @@
         local_rows, 3, head_cols
     )
     appended = jnp.stack([projected[:, 1], projected[:, 2]])
-    every_query = lax.all_gather(projected[:, 0], "dp", axis=0, tiled=True)
+    every_query = jnp.concatenate(
+        lax.all_to_all(jnp.stack([projected[:, 0]] * lax.axis_size("dp")), "dp", 0, 0), axis=0
+    )
     own_queries = projected[:, 0].reshape(local_rows, local_heads, HEAD_DIM).astype(jnp.float32)
     own_keys = projected[:, 1].reshape(local_rows, local_heads, HEAD_DIM).astype(jnp.float32)
     own_values = projected[:, 2].reshape(local_rows, local_heads, HEAD_DIM).astype(jnp.float32)

time: 379 us -> 365 us (0.963)
  blocking collectives: 80.4 us -> 55.5 us
  starting transfers between devices: 0.12 us -> 7.75 us
    all_gather x1 -> x0, blocking collectives: 24.7 us -> none  [body(): every_query = lax.all_gather(projected[:, 0], 'dp', axis=0, tiled=True)]
    all_to_all x0 -> x1, starting transfers between devices: none -> 7.62 us  [body(): lax.all_to_all(jnp.stack([projected[:, 0]] * lax.axis_size('dp')), 'dp',...]
    unnamed x22 -> x23, local copies, waits for them, and re-layouts: 18.4 us -> 18.5 us
  transfers between devices with their start and end apart: 3 -> 4, of which waited for: 3 -> 3; matrix products, arithmetic and copies ran while one was open for 1% -> 8% of each run, Pallas kernels for 0% -> 0%
where the time goes in v1:
time: 365 us; the launch traced here: 364 us
  waiting for transfers between devices  232 us (64%)
  blocking collectives  55.5 us (15%)
  local copies, waits for them, and re-layouts  33.8 us (9%)
  between operations  14 us (4%)
  matrix products  12.7 us (3%)
  starting transfers between devices  7.75 us (2%)
  other arithmetic  7.7 us (2%)
    unnamed x4, waiting for transfers between devices  94.6 us
    psum x1, waiting for transfers between devices, body(): lax.psum(jnp.dot(activated, w_down, preferred_element_type=jnp.float32),...  70.4 us
    psum x1, waiting for transfers between devices, body(): lax.psum(jnp.dot(context, w_out, preferred_element_type=jnp.float32), 'mp')  67.3 us
    pmax x1, blocking collectives, body(): global_max = lax.pmax(local_max, 'dp')  55.5 us
    unnamed x23, local copies, waits for them, and re-layouts  18.5 us
    all_to_all x1, starting transfers between devices, body(): lax.all_to_all(jnp.stack([projected[:, 0]] * lax.axis_size('dp')), 'dp',...  7.62 us
  transfers between devices with their start and end apart: 4, of which 3 were waited for; matrix products, arithmetic and copies ran while one was open for 8% of the time, Pallas kernels for 0%

profile of v1, /device:TPU:2, one launch (start us, length us, event | category | flops | bytes accessed | tf_op | source)
XLA Modules:
  0.0 363.8 jit_solution(1156278792572877418)
XLA Ops:
  7.2 1.5 copy.88
  8.7 0.9 fusion.9
  9.6 1.1 convolution_convert_fusion
  11.4 7.6 %all-to-all-start = ((bf16[32,16,128]{2,1,0:T(8,128)(2,1)}), bf16[32,16,128]{2,1,0:T(8,128)(2,1)S(1)}, u32[]{:S(2)}, u32[]{:S(2)}) async-start(bf16[32,16,128]{2,1,0:T(8,128)(2,1)} %stack.7), calls=%async_computation | async-start | bytes 262144 | tf_op jit(solution)/shard_map/all_to_all | solution.py:47
  20.4 0.8 iota_compare_fusion
  21.2 6.1 %fusion.35 = (bf16[1,128,128,128]{3,2,1,0:T(8,128)(2,1)}, bf16[1,128,128,128]{3,2,1,0:T(8,128)(2,1)}) fusion(bf16[2,128,128,128]{3,2,1,0:T(8,128)(2,1)} %param.18), kind=kLoop, calls=%fused_computation.70 | loop fusion | bytes 16777216 | tf_op jit(solution)/shard_map/slice | solution.py:60
  27.3 6.4 %copy.107 = bf16[1,128,128,128]{2,3,1,0:T(8,128)(2,1)} copy(bf16[1,128,128,128]{3,2,1,0:T(8,128)(2,1)} %get-tuple-element.9) | data formatting | bytes 8388608
  34.0 6.4 %copy.108 = bf16[1,128,128,128]{2,3,1,0:T(8,128)(2,1)} copy(bf16[1,128,128,128]{3,2,1,0:T(8,128)(2,1)} %get-tuple-element.8) | data formatting | bytes 8388608
  40.5 1.3 gather_fusion
  42.1 0.7 gather_fusion.1
  43.0 3.4 fusion.37
  47.1 55.5 %pmax.7 = f32[512,2]{0,1:T(2,128)S(1)} all-reduce(f32[512,2]{0,1:T(2,128)S(1)} %max.9), channel_id=1, replica_groups=mesh['dp'=32,'mp'=8] {'dp'}, use_global_device_ids=true, to_apply=%region_5.6 | all-reduce | flops 1024 | bytes 8192 | tf_op jit(solution)/shard_map/pmax | solution.py:94
  103.3 4.6 %fusion = f32[128,2,1,64]{3,2,1,0:T(1,128)S(1)} fusion(bf16[128,128,2,64]{1,3,2,0:T(8,128)(2,1)} %bitcast.73, bf16[128,2,128,1]{2,0,1,3:T(8,128)(2,1)S(1)} %get-tuple-element.10), kind=kOutput, calls=%fused_computation.8 | convolution fusion | flops 4194304 | bytes 4325376 | tf_op jit(solution)/shard_map/pht,pthd->phd/dot_general | solution.py:70
  109.3 0.8 maximum_multiply_fusion
  110.0 1.9 copy.102
  112.0 94.6 %reduce-scatter.4.cloned.1.call-done = f32[16,130]{1,0:T(8,128)} async-done(((f32[512,130]{1,0:T(8,128)}), f32[16,130]{1,0:T(8,128)}) %reduce-scatter.4.cloned.1.call-update) | async-done | bytes 8336
  208.2 1.8 fusion.38
  210.1 1.9 copy.112
  212.0 2.9 copy.97
  214.9 67.3 %all-reduce.3.cloned.1.call-done = f32[16,1024]{1,0:T(8,128)} async-done(((f32[16,1024]{1,0:T(8,128)}), f32[16,1024]{1,0:T(8,128)}) %all-reduce.3.cloned.1.call-update) | async-done | bytes 65552 | tf_op jit(solution)/shard_map/psum | solution.py:103
  282.2 0.8 fusion.12
  283.9 0.9 fusion.29
  285.4 70.4 %all-reduce.5.cloned.1.call-done = f32[16,1024]{1,0:T(8,128)} async-done(((f32[16,1024]{1,0:T(8,128)}), f32[16,1024]{1,0:T(8,128)}) %all-reduce.5.cloned.1.call-update) | async-done | bytes 65552 | tf_op jit(solution)/shard_map/psum | solution.py:115
  355.8 1.5 fusion.16
  (68 shorter events, 8.9 us)
Async XLA Ops:
  7.2 276.7 %copy-start = (bf16[512,1024]{1,0:T(8,128)(2,1)S(1)}, bf16[512,1024]{1,0:T(8,128)(2,1)}, u32[]{:S(2)}) copy-start(bf16[512,1024]{1,0:T(8,128)(2,1)} %param.17) | copy-start | bytes 3145732
  11.4 30.7 %all-to-all-start = ((bf16[32,16,128]{2,1,0:T(8,128)(2,1)}), bf16[32,16,128]{2,1,0:T(8,128)(2,1)S(1)}, u32[]{:S(2)}, u32[]{:S(2)}) async-start(bf16[32,16,128]{2,1,0:T(8,128)(2,1)} %stack.7), calls=%async_computation | async-start | bytes 262144 | tf_op jit(solution)/shard_map/all_to_all | solution.py:47
  19.0 187.6 %reduce-scatter.4.cloned.1.call-start = ((), (), s32[]{:S(2)}) async-start(), calls=%async_computation.4 | async-start | bytes 540672
  27.3 6.4 %copy-start.6 = (s32[128]{0:T(128)S(1)}, s32[128]{0:T(128)}, u32[]{:S(2)}) copy-start(s32[128]{0:T(128)} %param.21) | copy-start | bytes 1540
  34.0 6.5 %copy-start.1 = (s32[512]{0:T(512)S(1)}, s32[512]{0:T(512)}, u32[]{:S(2)}) copy-start(s32[512]{0:T(512)} %param.19) | copy-start | bytes 6148
  46.4 61.6 %copy-start.5 = (s32[128]{0:T(128)S(1)}, s32[128]{0:T(128)}, u32[]{:S(2)}) copy-start(s32[128]{0:T(128)} %param.20) | copy-start | bytes 1540
  103.3 106.8 %copy-start.2 = (bf16[1024,2,512]{2,1,0:T(2,128)(2,1)S(1)}, bf16[1024,2,512]{2,1,0:T(2,128)(2,1)}, u32[]{:S(2)}) copy-start(bf16[1024,2,512]{2,1,0:T(2,128)(2,1)} %param.16) | copy-start | bytes 6291460
  112.0 170.2 %all-reduce.3.cloned.1.call-start = ((), (), s32[]{:S(2)}) async-start(), calls=%async_computation.2 | async-start | bytes 131072 | tf_op jit(solution)/shard_map/psum | solution.py:103
  210.0 145.8 %all-reduce.5.cloned.1.call-start = ((), (), s32[]{:S(2)}) async-start(), calls=%async_computation.3 | async-start | bytes 131072 | tf_op jit(solution)/shard_map/psum | solution.py:115
  210.1 72.1 %copy-start.3 = (bf16[16,1024]{1,0:T(8,128)(2,1)S(1)}, bf16[16,1024]{1,0:T(8,128)(2,1)}, u32[]{:S(2)}) copy-start(bf16[16,1024]{1,0:T(8,128)(2,1)} %param.11) | copy-start | bytes 98308
  210.1 73.1 %copy-start.4 = (f32[1024]{0:T(1024)S(1)}, f32[1024]{0:T(1024)}, u32[]{:S(2)}) copy-start(f32[1024]{0:T(1024)} %param.15) | copy-start | bytes 12292
Sparse Core Ops, SparseCore 0:
  112.1 94.4 reduce-scatter.3
  210.1 72.0 all-reduce.2
  284.9 70.8 all-reduce.4
